TPU v7x, 32 devices: a whole 2x2x4 slice. The times are simulated.
32 devices in a mesh: groups: 2 (over y), gx: 4 (over z), gy: 2 (over x), gz: 2 (over core).
Axes of the slice: x: 2, y: 2, z: 4, core: 2. Of those that a mesh axis runs over, the one named last changes fastest.
Arguments:
- parent: bfloat16 [160, 32, 1024], P('groups', 'gx', ('gy', 'gz')), parts along dimension 0, may hold values from -6 to 6
- nest: bfloat16 [160, 24, 1536], P('groups', 'gx', ('gy', 'gz')), parts along dimension 0, may hold values from -6 to 6
- nu_parent: float32 [80], replicated, may hold values from 0.03 to 0.24
- nu_nest: float32 [80], replicated, may hold values from 0.03 to 0.24
- relax: float32 [80], replicated, may hold values from 0.1 to 0.5
- feedback: float32 [80], replicated, may hold values from 0.3 to 1
- vert_mix: float32 [80, 80], replicated, may hold values from -1 to 1
- fp_owner: int32 [4, 4, 256, 1], P('gx', ('gy', 'gz')), may hold values from 0 to 3; in each aligned block of 256 rows (0 to 255, 256 to 511, ..., all dimensions but the last counted through in order) at most 256 rows name the same one
- fp_cell: int32 [4, 4, 256], P('gx', ('gy', 'gz')), may hold values from 0 to 2047
- nest_of: int32 [24], replicated, may hold values from 0 to 2, as said below
Outputs:
- parent_out: bfloat16 [160, 32, 1024], P('groups', 'gx', ('gy', 'gz')), parts along dimension 0
- nest_out: bfloat16 [160, 24, 1536], P('groups', 'gx', ('gy', 'gz')), parts along dimension 0
There are 2 independent parts, one for each index of `groups`. A program takes and returns all parts, laid end to end along the dimension named above; an argument that names none is the same for every part. Nothing has to cross between parts.
Inputs may be any that keep to these rules, and one draw needn't show every extreme that they name: `fp_owner`: within the 256 blocks of one nest tile no parent tile is named more than 256 times; in some nest tiles one is named exactly 256 times. `nest_of`: never falls along the rows; every nest holds one or more rows; nest 1 holds rows 11 and 12.
All inputs are finite; a program needn't handle non-finite values.
Results may differ from a plain program's by a relative error of at most 0.0033.
Values may be sent and summed in bfloat16 or wider, within the bound.
No kernel may reach another device: no remote copies, remote signals or barrier semaphores. Data moves between devices by JAX's collectives and lax.ppermute only.
A program may use at most 64 MiB of HBM per device.

v0:
```python
import jax
import jax.numpy as jnp
from jax import lax
from jax.sharding import PartitionSpec as P

Y_AXES = ("gy", "gz")
HI = lax.Precision.HIGHEST


def shift_pairs(count):
    forward = [(i, i + 1) for i in range(count - 1)]
    backward = [(i + 1, i) for i in range(count - 1)]
    return (forward, backward)


def exchange(blocks):
    fwd_x, bwd_x = shift_pairs(lax.axis_size("gx"))
    fwd_y, bwd_y = shift_pairs(lax.axis_size(Y_AXES))
    last_rows = jnp.concatenate([b[:, -1, :] for b in blocks], axis=1)
    first_rows = jnp.concatenate([b[:, 0, :] for b in blocks], axis=1)
    last_cols = jnp.concatenate([b[:, :, -1] for b in blocks], axis=1)
    first_cols = jnp.concatenate([b[:, :, 0] for b in blocks], axis=1)
    above = lax.ppermute(last_rows, "gx", fwd_x)
    below = lax.ppermute(first_rows, "gx", bwd_x)
    left = lax.ppermute(last_cols, Y_AXES, fwd_y)
    right = lax.ppermute(first_cols, Y_AXES, bwd_y)
    out = []
    xo = 0
    yo = 0
    for b in blocks:
        w, h = (b.shape[2], b.shape[1])
        out.append(
            (
                above[:, xo : xo + w],
                below[:, xo : xo + w],
                left[:, yo : yo + h],
                right[:, yo : yo + h],
            )
        )
        xo += w
        yo += h
    return out


def per_row(values, rows, cols):
    if values.ndim == 1:
        return jnp.broadcast_to(values[:, None], (rows, cols)).reshape(rows * cols)
    return jnp.broadcast_to(values[:, :, None], values.shape + (cols,)).reshape(
        values.shape[0], rows * cols
    )


def flat_stencil(flat, rows, cols, halo, up_w=None, down_w=None):
    above, below, left, right = (h.astype(flat.dtype) for h in halo)
    levels = flat.shape[0]
    up = jnp.concatenate([above, flat[:, :-cols]], axis=1)
    down = jnp.concatenate([flat[:, cols:], below], axis=1)
    col = lax.broadcasted_iota(jnp.int32, (1, rows * cols), 1) % cols
    zero = jnp.zeros((levels, 1), flat.dtype)
    west = jnp.where(
        col == 0, per_row(left, rows, cols), jnp.concatenate([zero, flat[:, :-1]], axis=1)
    )
    east = jnp.where(
        col == cols - 1, per_row(right, rows, cols), jnp.concatenate([flat[:, 1:], zero], axis=1)
    )
    if down_w is not None:
        down = down * down_w[None, :]
        up = up * up_w[None, :]
    return down + up + east + west - 4.0 * flat


def mix_levels(matrix, flat):
    return jnp.dot(matrix, flat, precision=HI, preferred_element_type=jnp.float32)


def nest_segments(nest_of, first, count):
    index_rows = first + jnp.arange(count, dtype=jnp.int32)
    inside = (index_rows >= 0) & (index_rows < nest_of.shape[0])
    return jnp.where(inside, nest_of[jnp.clip(index_rows, 0, nest_of.shape[0] - 1)], -1)


def row_weights(segments):
    left_w = (segments[:-2] == segments[1:-1]).astype(jnp.float32)
    right_w = (segments[2:] == segments[1:-1]).astype(jnp.float32)
    return (left_w, right_w)


def block_expansion(block_rows, block_cols, rows, cols, zero):
    r = lax.broadcasted_iota(jnp.int32, (block_rows * block_cols, rows * cols), 0) + zero
    p = lax.broadcasted_iota(jnp.int32, (block_rows * block_cols, rows * cols), 1)
    hit = (p // cols // 3 == r // block_cols) & (p % cols // 3 == r % block_cols)
    return hit.astype(jnp.float32)


def body(parent, nest, nu_parent, nu_nest, relax, feedback, vert_mix, fp_owner, fp_cell, nest_of):
    levels, p_rows, p_cols = parent.shape
    _, n_rows, n_cols = nest.shape
    tiles_x = lax.axis_size("gx")
    here_x = lax.axis_index("gx")
    zero = jnp.minimum(here_x, 0)
    parent_halo, nest_halo = exchange([parent, nest])
    centre = parent.astype(jnp.float32).reshape(levels, p_rows * p_cols)
    stencil = flat_stencil(centre, p_rows, p_cols, parent_halo)
    flat_parent = mix_levels(vert_mix, centre + nu_parent[:, None] * stencil)
    owners = fp_owner.reshape(-1)
    cells = fp_cell.reshape(-1)
    requests = owners.shape[0]
    slots = 4 * requests // tiles_x
    owner_ids = jnp.arange(tiles_x, dtype=jnp.int32)
    if slots >= requests:
        chosen = owners[None, :] == owner_ids[:, None]
        wanted = jnp.where(chosen, cells[None, :], 0)
        wanted = jnp.pad(wanted, ((0, 0), (0, slots - requests))).reshape(-1)
    else:
        onehot = (owners[:, None] == owner_ids[None, :]).astype(jnp.int32)
        before = jnp.cumsum(onehot, axis=0) - onehot
        order_in = jnp.sum(before * onehot, axis=1)
        places = owners * slots + order_in
        wanted = jnp.zeros((tiles_x * slots,), jnp.int32).at[places].set(cells)
    served_ids = lax.all_to_all(wanted, "gx", split_axis=0, concat_axis=0, tiled=True)
    answers = lax.all_to_all(
        jnp.take(flat_parent, served_ids, axis=1), "gx", split_axis=1, concat_axis=1, tiled=True
    )
    if slots >= requests:
        answers = answers.reshape(levels, tiles_x, slots)[:, :, :requests]
        forcing_flat = answers[:, 0, :]
        for o in range(1, tiles_x):
            forcing_flat = jnp.where(chosen[o][None, :], answers[:, o, :], forcing_flat)
    else:
        forcing_flat = jnp.take(answers, places, axis=1)
    block_rows = n_rows // 3
    block_cols = n_cols // 3
    expand = block_expansion(block_rows, block_cols, n_rows, n_cols, zero)
    forcing_full = jnp.dot(forcing_flat, expand, precision=HI, preferred_element_type=jnp.float32)
    row_start = here_x * n_rows
    left_w, right_w = row_weights(nest_segments(nest_of, row_start - 1, n_rows + 2))
    up_w = per_row(left_w, n_rows, n_cols)
    down_w = per_row(right_w, n_rows, n_cols)
    nest_state = nest.astype(jnp.float32).reshape(levels, n_rows * n_cols)
    halo = nest_halo
    for turn_no in range(3):
        if turn_no > 0:
            shaped = nest_state.astype(jnp.bfloat16).reshape(levels, n_rows, n_cols)
            (halo,) = exchange([shaped])
        stencil_sum = flat_stencil(nest_state, n_rows, n_cols, halo, up_w, down_w)
        moved = nest_state + nu_nest[:, None] * stencil_sum
        moved = moved + relax[:, None] * (forcing_full - moved)
        nest_state = mix_levels(vert_mix, moved)
    block_sum = lax.dot_general(
        nest_state,
        expand,
        (((1,), (1,)), ((), ())),
        precision=HI,
        preferred_element_type=jnp.float32,
    )
    nudge_gap = block_sum / 9.0 - forcing_flat
    if slots >= requests:
        outgoing = jnp.where(chosen[None, :, :], nudge_gap[:, None, :], 0.0)
        outgoing = jnp.pad(outgoing, ((0, 0), (0, 0), (0, slots - requests)))
        outgoing = outgoing.reshape(levels, tiles_x * slots)
    else:
        outgoing = jnp.zeros((levels, tiles_x * slots), jnp.float32).at[:, places].set(nudge_gap)
    incoming = lax.all_to_all(outgoing, "gx", split_axis=1, concat_axis=1, tiled=True)
    summed = jnp.zeros_like(flat_parent).at[:, served_ids].add(incoming)
    parent_out = (flat_parent + feedback[:, None] * summed).astype(jnp.bfloat16)
    return (
        parent_out.reshape(levels, p_rows, p_cols),
        nest_state.astype(jnp.bfloat16).reshape(levels, n_rows, n_cols),
    )


def solution(mesh):
    placed = (
        P("groups", "gx", Y_AXES),
        P("groups", "gx", Y_AXES),
        P(),
        P(),
        P(),
        P(),
        P(),
        P("gx", Y_AXES, None, None),
        P("gx", Y_AXES, None),
        P(),
    )
    return jax.shard_map(
        body,
        mesh=mesh,
        in_specs=placed,
        out_specs=(P("groups", "gx", Y_AXES), P("groups", "gx", Y_AXES)),
        check_vma=False,
    )
```

profile of v0, /device:TPU:1, one launch (start us, length us, event | category | flops | bytes accessed | tf_op | source)
XLA Modules:
  0.0 121.2 jit_solution(3893287503478127455)
XLA Ops:
  3.5 1.4 %collective-permute-start = (bf16[80,640]{1,0:T(8,128)(2,1)}, bf16[80,640]{1,0:T(8,128)(2,1)}, u32[]{:S(2)}, u32[]{:S(2)}) collective-permute-start(bf16[80,640]{1,0:T(8,128)(2,1)} %pad_maximum_fusion), channel_id=1, source_target_pairs={{4,0},{8,4},{12,8},{5,1},{9,5},{13,9},{6,2},{10,6},{14,10},{7,3},{... | collective-permute-start | bytes 307208 | tf_op jit(solution)/shard_map/ppermute | solution.py:24
  5.6 5.3 %collective-permute-start.1 = (bf16[80,640]{1,0:T(8,128)(2,1)}, bf16[80,640]{1,0:T(8,128)(2,1)}, u32[]{:S(2)}, u32[]{:S(2)}) collective-permute-start(bf16[80,640]{1,0:T(8,128)(2,1)} %pad_maximum_fusion.1), channel_id=1, source_target_pairs={{0,4},{4,8},{8,12},{1,5},{5,9},{9,13},{2,6},{6,10},{10,14},{3,7},{... | collective-permute-start | bytes 307208 | tf_op jit(solution)/shard_map/ppermute | solution.py:23
  11.4 4.4 %collective-permute-start.3 = (bf16[80,14]{0,1:T(8,128)(2,1)S(1)}, bf16[80,14]{0,1:T(8,128)(2,1)S(1)}, u32[]{:S(2)}, u32[]{:S(2)}) collective-permute-start(bf16[80,14]{0,1:T(8,128)(2,1)S(1)} %pad_maximum_fusion.3), channel_id=1, source_target_pairs={{0,1},{1,2},{2,3},{4,5},{5,6},{6,7},{8,9},{9,10},{10,11},{12,13},{... | collective-permute-start | bytes 6728 | tf_op jit(solution)/shard_map/ppermute | solution.py:25
  16.1 1.9 %collective-permute-start.2 = (bf16[80,14]{0,1:T(8,128)(2,1)S(1)}, bf16[80,14]{0,1:T(8,128)(2,1)S(1)}, u32[]{:S(2)}, u32[]{:S(2)}) collective-permute-start(bf16[80,14]{0,1:T(8,128)(2,1)S(1)} %pad_maximum_fusion.2), channel_id=1, source_target_pairs={{1,0},{2,1},{3,2},{5,4},{6,5},{7,6},{9,8},{10,9},{11,10},{13,12},{... | collective-permute-start | bytes 6728 | tf_op jit(solution)/shard_map/ppermute | solution.py:26
  18.7 3.6 %all-to-all-start = ((s32[4,256,1]{1,2,0:T(1,128)}), s32[4,256,1]{1,2,0:T(1,128)S(1)}, u32[]{:S(2)}, u32[]{:S(2)}) async-start(s32[4,256,1]{1,2,0:T(1,128)} %compare_select_fusion.1), calls=%async_computation | async-start | bytes 8192 | tf_op jit(solution)/shard_map/all_to_all | solution.py:120
  25.0 1.4 %fusion.134 = (f32[80,2303]{1,0:T(8,128)}, f32[80,2303]{1,0:T(8,128)}) fusion(f32[80,2304]{1,0:T(8,128)S(1)} %bitcast.111), kind=kLoop, calls=%fused_computation.210 | loop fusion | bytes 2947840 | tf_op jit(solution)/shard_map/slice | solution.py:64
  27.2 2.2 %fusion.6 = pred[256,2304]{1,0:T(32,128)(4,1)} fusion(s32[256]{0:T(256)S(1)} %get-tuple-element.58, s32[256]{0:T(256)S(1)} %get-tuple-element.59, s32[2304]{0:T(1024)S(1)} %get-tuple-element.62, s32[2304]{0:T(1024)S(1)} %get-tuple-element.63, s32[256]{0:T(256)S(1)} %get-tuple-element.57, s32[256]{0:T(256)S(1)} %get-tuple-element.60, ...), kind=kLoop, calls=%fused_computation.20 | loop fusion | flops 13565952 | bytes 635904 | tf_op jit(solution)/shard_map/and | solution.py:91
  33.8 2.8 %convolution_bitcast_fusion.2 = f32[80,2048]{1,0:T(8,128)S(1)} fusion(f32[80,80]{1,0:T(8,128)S(1)} %copy-done, f32[80,2048]{1,0:T(8,128)S(1)} %bitcast.115, f32[80,256]{1,0:T(8,128)S(1)} %slice_convert_fusion.3, f32[80,1792]{1,0:T(8,128)} %get-tuple-element.28, f32[80,1792]{1,0:T(8,128)} %get-tuple-element.27, f32[80,256]{1,0:T(8,128)S(1)} %slice_convert_fusion.2, ...), kind=kOutput, calls=%fused_computation.13 | convolution fusion | flops 159088640 | bytes 5272256 | tf_op jit(solution)/shard_map/dot_general | solution.py:73
  36.9 2.8 %gather_fusion.1 = f32[1024,80]{1,0:T(8,128)S(1)} fusion(f32[80,2048]{0,1:T(8,128)S(1)} %copy.93, s32[1024]{0:T(1024)S(1)} %broadcast_clamp_fusion), kind=kCustom, calls=%fused_computation.1 | custom fusion | bytes 659456 | tf_op jit(solution)/shard_map/jit(_take)/gather | solution.py:122
  40.7 4.5 %all-to-all-start.1 = ((f32[80,4,256]{2,0,1:T(8,128)}), f32[80,4,256]{2,0,1:T(8,128)S(1)}, u32[]{:S(2)}, u32[]{:S(2)}) async-start(f32[80,4,256]{2,0,1:T(8,128)} %broadcast_select_fusion.1), calls=%async_computation.1 | async-start | bytes 655360 | tf_op jit(solution)/shard_map/all_to_all | solution.py:121
  47.8 1.5 %slice_convert_fusion = f32[80,384]{1,0:T(8,128)} fusion(bf16[80,640]{1,0:T(8,128)(2,1)} %collective-permute-done.1), kind=kLoop, calls=%fused_computation.131 | loop fusion | flops 30720 | bytes 184320 | tf_op jit(solution)/shard_map/convert_element_type | solution.py:54
  49.3 1.6 %slice_convert_fusion.1 = f32[80,384]{1,0:T(8,128)} fusion(bf16[80,640]{1,0:T(8,128)(2,1)} %collective-permute-done), kind=kLoop, calls=%fused_computation.132 | loop fusion | flops 30720 | bytes 184320 | tf_op jit(solution)/shard_map/convert_element_type | solution.py:54
  50.8 3.9 %all-to-all-done.1 = f32[80,4,256]{2,0,1:T(8,128)S(1)} async-done(((f32[80,4,256]{2,0,1:T(8,128)}), f32[80,4,256]{2,0,1:T(8,128)S(1)}, u32[]{:S(2)}, u32[]{:S(2)}) %all-to-all-start.1) | async-done | bytes 327712 | tf_op jit(solution)/shard_map/all_to_all | solution.py:121
  55.7 3.3 %fusion.145 = (bf16[80,2304]{1,0:T(8,128)(2,1)S(1)}, f32[80,2304]{1,0:T(8,128)S(1)}) fusion(f32[80,80]{1,0:T(8,128)S(1)} %copy-done, f32[80,2304]{1,0:T(8,128)S(1)} %fusion.148, f32[80,2304]{1,0:T(8,128)S(1)} %bitcast.112, f32[80,1920]{1,0:T(8,128)} %get-tuple-element.23, f32[80,384]{1,0:T(8,128)S(1)} %copy-done.16, f32[80,384]{1,0:T(8,128)S(1)} %copy-done.17, ...), kind=kOutput, calls=%fused_computation.221 | convolution fusion | flops 180080640 | bytes 7052800 | tf_op jit(solution)/shard_map/dot_general | solution.py:73
  62.5 4.4 %collective-permute-start.7 = (bf16[80,6]{0,1:T(8,128)(2,1)S(1)}, bf16[80,6]{0,1:T(8,128)(2,1)S(1)}, u32[]{:S(2)}, u32[]{:S(2)}) collective-permute-start(bf16[80,6]{0,1:T(8,128)(2,1)S(1)} %bitcast.154), channel_id=1, source_target_pairs={{0,1},{1,2},{2,3},{4,5},{5,6},{6,7},{8,9},{9,10},{10,11},{12,13},{... | collective-permute-start | bytes 2888 | tf_op jit(solution)/shard_map/ppermute | solution.py:25
  68.2 1.9 %collective-permute-start.6 = (bf16[80,6]{0,1:T(8,128)(2,1)S(1)}, bf16[80,6]{0,1:T(8,128)(2,1)S(1)}, u32[]{:S(2)}, u32[]{:S(2)}) collective-permute-start(bf16[80,6]{0,1:T(8,128)(2,1)S(1)} %bitcast.156), channel_id=1, source_target_pairs={{1,0},{2,1},{3,2},{5,4},{6,5},{7,6},{9,8},{10,9},{11,10},{13,12},{... | collective-permute-start | bytes 2888 | tf_op jit(solution)/shard_map/ppermute | solution.py:26
  77.0 4.9 %collective-permute-start.9 = (bf16[80,384]{1,0:T(8,128)(2,1)S(1)}, bf16[80,384]{1,0:T(8,128)(2,1)}, u32[]{:S(2)}, u32[]{:S(2)}) collective-permute-start(bf16[80,384]{1,0:T(8,128)(2,1)S(1)} %bitcast.143), channel_id=1, source_target_pairs={{0,4},{4,8},{8,12},{1,5},{5,9},{9,13},{2,6},{6,10},{10,14},{3,7},{... | collective-permute-start | bytes 184328 | tf_op jit(solution)/shard_map/ppermute | solution.py:23
  82.5 1.5 %collective-permute-start.8 = (bf16[80,384]{1,0:T(8,128)(2,1)}, bf16[80,384]{1,0:T(8,128)(2,1)}, u32[]{:S(2)}, u32[]{:S(2)}) collective-permute-start(bf16[80,384]{1,0:T(8,128)(2,1)} %bitcast.105), channel_id=1, source_target_pairs={{4,0},{8,4},{12,8},{5,1},{9,5},{13,9},{6,2},{10,6},{14,10},{7,3},{... | collective-permute-start | bytes 184328 | tf_op jit(solution)/shard_map/ppermute | solution.py:24
  84.2 3.3 %collective-permute-start.11 = (bf16[80,6]{0,1:T(8,128)(2,1)S(1)}, bf16[80,6]{0,1:T(8,128)(2,1)S(1)}, u32[]{:S(2)}, u32[]{:S(2)}) collective-permute-start(bf16[80,6]{0,1:T(8,128)(2,1)S(1)} %bitcast.155), channel_id=1, source_target_pairs={{0,1},{1,2},{2,3},{4,5},{5,6},{6,7},{8,9},{9,10},{10,11},{12,13},{... | collective-permute-start | bytes 2888 | tf_op jit(solution)/shard_map/ppermute | solution.py:25
  87.9 1.9 %collective-permute-start.10 = (bf16[80,6]{0,1:T(8,128)(2,1)S(1)}, bf16[80,6]{0,1:T(8,128)(2,1)S(1)}, u32[]{:S(2)}, u32[]{:S(2)}) collective-permute-start(bf16[80,6]{0,1:T(8,128)(2,1)S(1)} %bitcast.157), channel_id=1, source_target_pairs={{1,0},{2,1},{3,2},{5,4},{6,5},{7,6},{9,8},{10,9},{11,10},{13,12},{... | collective-permute-start | bytes 2888 | tf_op jit(solution)/shard_map/ppermute | solution.py:26
  95.1 1.3 %fusion.147 = (bf16[2304,80]{0,1:T(8,128)(2,1)S(1)}, f32[2304,80]{0,1:T(8,128)S(1)}) fusion(f32[80,80]{1,0:T(8,128)S(1)} %copy-done, f32[80,2304]{1,0:T(8,128)S(1)} %fusion.148, f32[80,2304]{1,0:T(8,128)S(1)} %get-tuple-element.50, f32[80,1920]{1,0:T(8,128)S(1)} %copy-done.10, f32[80,384]{1,0:T(8,128)S(1)} %convert_element_type.89, ...), kind=kOutput, calls=%fused_computation.223 | convolution fusion | flops 180080640 | bytes 7052800 | tf_op jit(solution)/shard_map/dot_general | solution.py:73
  98.5 4.7 %all-to-all-start.2 = ((f32[80,4,256]{2,0,1:T(8,128)}), f32[80,4,256]{2,0,1:T(8,128)S(1)}, u32[]{:S(2)}, u32[]{:S(2)}) async-start(f32[80,4,256]{2,0,1:T(8,128)} %broadcast_select_fusion), calls=%async_computation.2 | async-start | bytes 655360 | tf_op jit(solution)/shard_map/all_to_all | solution.py:163
  103.9 8.7 %all-to-all-done.2 = f32[80,4,256]{2,0,1:T(8,128)S(1)} async-done(((f32[80,4,256]{2,0,1:T(8,128)}), f32[80,4,256]{2,0,1:T(8,128)S(1)}, u32[]{:S(2)}, u32[]{:S(2)}) %all-to-all-start.2) | async-done | bytes 327712 | tf_op jit(solution)/shard_map/all_to_all | solution.py:163
  112.9 6.3 %scatter_custom_fusion = f32[80,2048]{0,1:T(8,128)S(1)} fusion(s32[1024]{0:T(1024)S(1)} %bitcast.147, f32[1024,80]{1,0:T(8,128)S(1)} %copy.109, f32[]{:T(128)} %constant.109.clone.1), kind=kCustom, calls=%fused_computation.92 | custom fusion | flops 81920 | bytes 655364 | tf_op jit(solution)/shard_map/scatter-add | solution.py:164
  (172 shorter events, 40.3 us)
Async XLA Ops:
  0.6 33.1 %copy-start = (f32[80,80]{1,0:T(8,128)S(1)}, f32[80,80]{1,0:T(8,128)}, u32[]{:S(2)}) copy-start(f32[80,80]{1,0:T(8,128)} %param.16) | copy-start | bytes 76804
  0.6 10.2 %copy-start.15 = (bf16[80,6,384]{2,0,1:T(8,128)(2,1)S(1)}, bf16[80,6,384]{2,0,1:T(8,128)(2,1)}, u32[]{:S(2)}) copy-start(bf16[80,6,384]{2,0,1:T(8,128)(2,1)} %param.11) | copy-start | bytes 1105924
  0.7 10.3 %copy-start.14 = (bf16[80,8,256]{2,1,0:T(8,128)(2,1)S(1)}, bf16[80,8,256]{2,1,0:T(8,128)(2,1)}, u32[]{:S(2)}) copy-start(bf16[80,8,256]{2,1,0:T(8,128)(2,1)} %param.10) | copy-start | bytes 983044
  3.5 14.6 %copy-start.20 = (s32[1,1,256,1]{2,3,1,0:T(1,128)S(1)}, s32[1,1,256,1]{2,3,1,0:T(1,128)}, u32[]{:S(2)}) copy-start(s32[1,1,256,1]{2,3,1,0:T(1,128)} %param.17) | copy-start | bytes 3076
  3.5 14.6 %copy-start.21 = (s32[1,1,256]{2,1,0:T(1,128)S(1)}, s32[1,1,256]{2,1,0:T(1,128)}, u32[]{:S(2)}) copy-start(s32[1,1,256]{2,1,0:T(1,128)} %param.18) | copy-start | bytes 3076
  3.5 28.7 %collective-permute-start = (bf16[80,640]{1,0:T(8,128)(2,1)}, bf16[80,640]{1,0:T(8,128)(2,1)}, u32[]{:S(2)}, u32[]{:S(2)}) collective-permute-start(bf16[80,640]{1,0:T(8,128)(2,1)} %pad_maximum_fusion), channel_id=1, source_target_pairs={{4,0},{8,4},{12,8},{5,1},{9,5},{13,9},{6,2},{10,6},{14,10},{7,3},{... | collective-permute-start | bytes 307208 | tf_op jit(solution)/shard_map/ppermute | solution.py:24
  5.6 27.4 %collective-permute-start.1 = (bf16[80,640]{1,0:T(8,128)(2,1)}, bf16[80,640]{1,0:T(8,128)(2,1)}, u32[]{:S(2)}, u32[]{:S(2)}) collective-permute-start(bf16[80,640]{1,0:T(8,128)(2,1)} %pad_maximum_fusion.1), channel_id=1, source_target_pairs={{0,4},{4,8},{8,12},{1,5},{5,9},{9,13},{2,6},{6,10},{10,14},{3,7},{... | collective-permute-start | bytes 307208 | tf_op jit(solution)/shard_map/ppermute | solution.py:23
  11.4 18.1 %collective-permute-start.3 = (bf16[80,14]{0,1:T(8,128)(2,1)S(1)}, bf16[80,14]{0,1:T(8,128)(2,1)S(1)}, u32[]{:S(2)}, u32[]{:S(2)}) collective-permute-start(bf16[80,14]{0,1:T(8,128)(2,1)S(1)} %pad_maximum_fusion.3), channel_id=1, source_target_pairs={{0,1},{1,2},{2,3},{4,5},{5,6},{6,7},{8,9},{9,10},{10,11},{12,13},{... | collective-permute-start | bytes 6728 | tf_op jit(solution)/shard_map/ppermute | solution.py:25
  16.1 13.4 %collective-permute-start.2 = (bf16[80,14]{0,1:T(8,128)(2,1)S(1)}, bf16[80,14]{0,1:T(8,128)(2,1)S(1)}, u32[]{:S(2)}, u32[]{:S(2)}) collective-permute-start(bf16[80,14]{0,1:T(8,128)(2,1)S(1)} %pad_maximum_fusion.2), channel_id=1, source_target_pairs={{1,0},{2,1},{3,2},{5,4},{6,5},{7,6},{9,8},{10,9},{11,10},{13,12},{... | collective-permute-start | bytes 6728 | tf_op jit(solution)/shard_map/ppermute | solution.py:26
  18.7 13.4 %all-to-all-start = ((s32[4,256,1]{1,2,0:T(1,128)}), s32[4,256,1]{1,2,0:T(1,128)S(1)}, u32[]{:S(2)}, u32[]{:S(2)}) async-start(s32[4,256,1]{1,2,0:T(1,128)} %compare_select_fusion.1), calls=%async_computation | async-start | bytes 8192 | tf_op jit(solution)/shard_map/all_to_all | solution.py:120
  40.7 14.1 %all-to-all-start.1 = ((f32[80,4,256]{2,0,1:T(8,128)}), f32[80,4,256]{2,0,1:T(8,128)S(1)}, u32[]{:S(2)}, u32[]{:S(2)}) async-start(f32[80,4,256]{2,0,1:T(8,128)} %broadcast_select_fusion.1), calls=%async_computation.1 | async-start | bytes 655360 | tf_op jit(solution)/shard_map/all_to_all | solution.py:121
  46.8 8.0 %copy-start.4 = (pred[256,2304]{1,0:T(32,128)(4,1)S(1)}, pred[256,2304]{1,0:T(32,128)(4,1)}, u32[]{:S(2)}) copy-start(pred[256,2304]{1,0:T(32,128)(4,1)} %fusion.6) | copy-start | bytes 1769476
  49.3 6.4 %copy-start.6 = (f32[80,2303]{1,0:T(8,128)S(1)}, f32[80,2303]{1,0:T(8,128)}, u32[]{:S(2)}) copy-start(f32[80,2303]{1,0:T(8,128)} %get-tuple-element.21) | copy-start | bytes 2210884
  49.3 6.4 %copy-start.18 = (f32[80]{0:T(128)S(1)}, f32[80]{0:T(128)}, u32[]{:S(2)}) copy-start(f32[80]{0:T(128)} %param.14) | copy-start | bytes 964
  49.3 6.4 %copy-start.19 = (f32[80]{0:T(128)S(1)}, f32[80]{0:T(128)}, u32[]{:S(2)}) copy-start(f32[80]{0:T(128)} %param.13) | copy-start | bytes 964
  59.7 13.8 %collective-permute-start.5 = (bf16[80,384]{1,0:T(8,128)(2,1)S(1)}, bf16[80,384]{1,0:T(8,128)(2,1)S(1)}, u32[]{:S(2)}, u32[]{:S(2)}) collective-permute-start(bf16[80,384]{1,0:T(8,128)(2,1)S(1)} %bitcast.142), channel_id=1, source_target_pairs={{0,4},{4,8},{8,12},{1,5},{5,9},{9,13},{2,6},{6,10},{10,14},{3,7},{... | collective-permute-start | bytes 184328 | tf_op jit(solution)/shard_map/ppermute | solution.py:23
  61.1 12.5 %collective-permute-start.4 = (bf16[80,384]{1,0:T(8,128)(2,1)S(1)}, bf16[80,384]{1,0:T(8,128)(2,1)S(1)}, u32[]{:S(2)}, u32[]{:S(2)}) collective-permute-start(bf16[80,384]{1,0:T(8,128)(2,1)S(1)} %bitcast.144), channel_id=1, source_target_pairs={{4,0},{8,4},{12,8},{5,1},{9,5},{13,9},{6,2},{10,6},{14,10},{7,3},{... | collective-permute-start | bytes 184328 | tf_op jit(solution)/shard_map/ppermute | solution.py:24
  62.5 8.7 %collective-permute-start.7 = (bf16[80,6]{0,1:T(8,128)(2,1)S(1)}, bf16[80,6]{0,1:T(8,128)(2,1)S(1)}, u32[]{:S(2)}, u32[]{:S(2)}) collective-permute-start(bf16[80,6]{0,1:T(8,128)(2,1)S(1)} %bitcast.154), channel_id=1, source_target_pairs={{0,1},{1,2},{2,3},{4,5},{5,6},{6,7},{8,9},{9,10},{10,11},{12,13},{... | collective-permute-start | bytes 2888 | tf_op jit(solution)/shard_map/ppermute | solution.py:25
  68.2 4.9 %collective-permute-start.6 = (bf16[80,6]{0,1:T(8,128)(2,1)S(1)}, bf16[80,6]{0,1:T(8,128)(2,1)S(1)}, u32[]{:S(2)}, u32[]{:S(2)}) collective-permute-start(bf16[80,6]{0,1:T(8,128)(2,1)S(1)} %bitcast.156), channel_id=1, source_target_pairs={{1,0},{2,1},{3,2},{5,4},{6,5},{7,6},{9,8},{10,9},{11,10},{13,12},{... | collective-permute-start | bytes 2888 | tf_op jit(solution)/shard_map/ppermute | solution.py:26
  77.0 16.3 %collective-permute-start.9 = (bf16[80,384]{1,0:T(8,128)(2,1)S(1)}, bf16[80,384]{1,0:T(8,128)(2,1)}, u32[]{:S(2)}, u32[]{:S(2)}) collective-permute-start(bf16[80,384]{1,0:T(8,128)(2,1)S(1)} %bitcast.143), channel_id=1, source_target_pairs={{0,4},{4,8},{8,12},{1,5},{5,9},{9,13},{2,6},{6,10},{10,14},{3,7},{... | collective-permute-start | bytes 184328 | tf_op jit(solution)/shard_map/ppermute | solution.py:23
  82.5 11.7 %collective-permute-start.8 = (bf16[80,384]{1,0:T(8,128)(2,1)}, bf16[80,384]{1,0:T(8,128)(2,1)}, u32[]{:S(2)}, u32[]{:S(2)}) collective-permute-start(bf16[80,384]{1,0:T(8,128)(2,1)} %bitcast.105), channel_id=1, source_target_pairs={{4,0},{8,4},{12,8},{5,1},{9,5},{13,9},{6,2},{10,6},{14,10},{7,3},{... | collective-permute-start | bytes 184328 | tf_op jit(solution)/shard_map/ppermute | solution.py:24
  84.2 6.8 %collective-permute-start.11 = (bf16[80,6]{0,1:T(8,128)(2,1)S(1)}, bf16[80,6]{0,1:T(8,128)(2,1)S(1)}, u32[]{:S(2)}, u32[]{:S(2)}) collective-permute-start(bf16[80,6]{0,1:T(8,128)(2,1)S(1)} %bitcast.155), channel_id=1, source_target_pairs={{0,1},{1,2},{2,3},{4,5},{5,6},{6,7},{8,9},{9,10},{10,11},{12,13},{... | collective-permute-start | bytes 2888 | tf_op jit(solution)/shard_map/ppermute | solution.py:25
  87.9 4.9 %collective-permute-start.10 = (bf16[80,6]{0,1:T(8,128)(2,1)S(1)}, bf16[80,6]{0,1:T(8,128)(2,1)S(1)}, u32[]{:S(2)}, u32[]{:S(2)}) collective-permute-start(bf16[80,6]{0,1:T(8,128)(2,1)S(1)} %bitcast.157), channel_id=1, source_target_pairs={{1,0},{2,1},{3,2},{5,4},{6,5},{7,6},{9,8},{10,9},{11,10},{13,12},{... | collective-permute-start | bytes 2888 | tf_op jit(solution)/shard_map/ppermute | solution.py:26
  98.5 14.2 %all-to-all-start.2 = ((f32[80,4,256]{2,0,1:T(8,128)}), f32[80,4,256]{2,0,1:T(8,128)S(1)}, u32[]{:S(2)}, u32[]{:S(2)}) async-start(f32[80,4,256]{2,0,1:T(8,128)} %broadcast_select_fusion), calls=%async_computation.2 | async-start | bytes 655360 | tf_op jit(solution)/shard_map/all_to_all | solution.py:163
  (15 other events, 24.0 us)
where the time goes:
time: 122 us; the launch traced here: 121 us
  starting transfers between devices  46.3 us (38%)
  local copies, waits for them, and re-layouts  30.1 us (25%)
  other arithmetic  18.7 us (15%)
  waiting for transfers between devices  13.9 us (11%)
  matrix products  10.8 us (9%)
  between operations  1.45 us (1%)
    ppermute x3, starting transfers between devices, exchange(): left = lax.ppermute(last_cols, Y_AXES, fwd_y)  12.1 us
    ppermute x3, starting transfers between devices, exchange(): above = lax.ppermute(last_rows, 'gx', fwd_x)  11.5 us
    unnamed x68, local copies, waits for them, and re-layouts  10.8 us
    all_to_all x1, waiting for transfers between devices, body(): lax.all_to_all(outgoing, 'gx', split_axis=1, concat_axis=1, tiled=True)  8.71 us
    dot_general x4, matrix products, mix_levels(): jnp.dot(matrix, flat, precision=HI, preferred_element_type=jnp.float32)  8.71 us
    convert_element_type x12, other arithmetic, flat_stencil(): above, below, left, right = (h.astype(flat.dtype) for h in halo)  6.43 us
    scatter-add x1, other arithmetic, body(): summed = jnp.zeros_like(flat_parent).at[:, served_ids].add(incoming)  6.28 us
    ppermute x3, starting transfers between devices, exchange(): right = lax.ppermute(first_cols, Y_AXES, bwd_y)  5.74 us
  transfers between devices with their start and end apart: 15, of which 4 were waited for; matrix products, arithmetic and copies ran while one was open for 23% of the time, Pallas kernels for 0%

commit v1 on v0

--- a/solution.py
+++ b/solution.py
@@ -5,6 +5,18 @@
 
 Y_AXES = ("gy", "gz")
 HI = lax.Precision.HIGHEST
+
+
+def cut_along(x, dim, size):
+    shape = x.shape
+    tiles = x.reshape(*shape[:dim], size, shape[dim] // size, *shape[dim + 1 :])
+    return jnp.moveaxis(tiles, dim, 0)
+
+
+def in_order(pieces, dim):
+    shape = list(pieces.shape[1:])
+    shape[dim] *= pieces.shape[0]
+    return jnp.moveaxis(pieces, 0, dim).reshape(shape)
 
 
 def shift_pairs(count):
@@ -118,9 +130,15 @@
         places = owners * slots + order_in
         wanted = jnp.zeros((tiles_x * slots,), jnp.int32).at[places].set(cells)
     served_ids = lax.all_to_all(wanted, "gx", split_axis=0, concat_axis=0, tiled=True)
-    answers = lax.all_to_all(
-        jnp.take(flat_parent, served_ids, axis=1), "gx", split_axis=1, concat_axis=1, tiled=True
-    )
+    value = jnp.take(flat_parent, served_ids, axis=1)
+    length, index = (lax.axis_size("gx"), lax.axis_index("gx"))
+    pieces = cut_along(value, 1, length)
+    gathered = [pieces[index]]
+    for step in range(1, length):
+        sent = pieces[index ^ step]
+        gathered.append(lax.ppermute(sent, "gx", [(i_2, i_2 ^ step) for i_2 in range(length)]))
+    pieces = jnp.stack(gathered)[index ^ jnp.arange(length)]
+    answers = in_order(pieces, 1)
     if slots >= requests:
         answers = answers.reshape(levels, tiles_x, slots)[:, :, :requests]
         forcing_flat = answers[:, 0, :]

time: 122 us -> 118 us (0.967)
  other arithmetic: 18.7 us -> 11.8 us
  local copies, waits for them, and re-layouts: 30.1 us -> 32.6 us
    convert_element_type x12, other arithmetic: 6.43 us -> 1.39 us  [flat_stencil(): above, below, left, right = (h.astype(flat.dtype) for h in halo)]
    all_to_all x1 -> x0, starting transfers between devices: 4.54 us -> none  [body(): lax.all_to_all(jnp.take(flat_parent, served_ids, axis=1), 'gx', split_axi...]
    all_to_all x1 -> x0, waiting for transfers between devices: 3.94 us -> none  [body(): lax.all_to_all(jnp.take(flat_parent, served_ids, axis=1), 'gx', split_axi...]
    ppermute x0 -> x3, starting transfers between devices: none -> 3.76 us  [body(): lax.ppermute(sent, 'gx', [(i_2, i_2 ^ step) for i_2 in range(length)])]
    ppermute x0 -> x3, waiting for transfers between devices: none -> 3.65 us  [body(): lax.ppermute(sent, 'gx', [(i_2, i_2 ^ step) for i_2 in range(length)])]
    ppermute x3, starting transfers between devices: 5.74 us -> 8.84 us  [exchange(): right = lax.ppermute(first_cols, Y_AXES, bwd_y)]
    slice x6, local copies, waits for them, and re-layouts: 0.79 us -> 2.83 us  [exchange(): first_cols = jnp.concatenate([b[:, :, 0] for b in blocks], axis=1)]
    all_to_all x1, starting transfers between devices: 3.58 us -> 5.38 us  [body(): lax.all_to_all(wanted, 'gx', split_axis=0, concat_axis=0, tiled=True)]
  transfers between devices with their start and end apart: 15 -> 17, of which waited for: 4 -> 3; matrix products, arithmetic and copies ran while one was open for 23% -> 20% of each run, Pallas kernels for 0% -> 0%
where the time goes in v1:
time: 118 us; the launch traced here: 117 us
  starting transfers between devices  47 us (40%)
  local copies, waits for them, and re-layouts  32.6 us (28%)
  waiting for transfers between devices  13.3 us (11%)
  other arithmetic  11.8 us (10%)
  matrix products  10.3 us (9%)
  between operations  1.66 us (1%)
    unnamed x80, local copies, waits for them, and re-layouts  12.5 us
    ppermute x3, starting transfers between devices, exchange(): above = lax.ppermute(last_rows, 'gx', fwd_x)  11.4 us
    ppermute x3, starting transfers between devices, exchange(): left = lax.ppermute(last_cols, Y_AXES, fwd_y)  10.3 us
    all_to_all x1, waiting for transfers between devices, body(): lax.all_to_all(outgoing, 'gx', split_axis=1, concat_axis=1, tiled=True)  9.6 us
    ppermute x3, starting transfers between devices, exchange(): right = lax.ppermute(first_cols, Y_AXES, bwd_y)  8.84 us
    dot_general x4, matrix products, mix_levels(): jnp.dot(matrix, flat, precision=HI, preferred_element_type=jnp.float32)  8.25 us
    scatter-add x1, other arithmetic, body(): summed = jnp.zeros_like(flat_parent).at[:, served_ids].add(incoming)  6.28 us
    all_to_all x1, starting transfers between devices, body(): lax.all_to_all(wanted, 'gx', split_axis=0, concat_axis=0, tiled=True)  5.38 us
  transfers between devices with their start and end apart: 17, of which 3 were waited for; matrix products, arithmetic and copies ran while one was open for 20% of the time, Pallas kernels for 0%

profile of v1, /device:TPU:1, one launch (start us, length us, event | category | flops | bytes accessed | tf_op | source)
XLA Modules:
  0.0 116.8 jit_solution(15939586031200092001)
XLA Ops:
  3.3 1.9 %collective-permute-start.2 = (bf16[80,14]{0,1:T(8,128)(2,1)S(1)}, bf16[80,14]{0,1:T(8,128)(2,1)S(1)}, u32[]{:S(2)}, u32[]{:S(2)}) collective-permute-start(bf16[80,14]{0,1:T(8,128)(2,1)S(1)} %pad_maximum_fusion.3), channel_id=1, source_target_pairs={{1,0},{2,1},{3,2},{5,4},{6,5},{7,6},{9,8},{10,9},{11,10},{13,12},{... | collective-permute-start | bytes 6728 | tf_op jit(solution)/shard_map/ppermute | solution.py:38
  5.5 4.5 %collective-permute-start.3 = (bf16[80,14]{0,1:T(8,128)(2,1)S(1)}, bf16[80,14]{0,1:T(8,128)(2,1)S(1)}, u32[]{:S(2)}, u32[]{:S(2)}) collective-permute-start(bf16[80,14]{0,1:T(8,128)(2,1)S(1)} %pad_maximum_fusion.4), channel_id=1, source_target_pairs={{0,1},{1,2},{2,3},{4,5},{5,6},{6,7},{8,9},{9,10},{10,11},{12,13},{... | collective-permute-start | bytes 6728 | tf_op jit(solution)/shard_map/ppermute | solution.py:37
  10.2 3.2 %collective-permute-start.1 = (bf16[80,640]{1,0:T(8,128)(2,1)S(1)}, bf16[80,640]{1,0:T(8,128)(2,1)S(1)}, u32[]{:S(2)}, u32[]{:S(2)}) collective-permute-start(bf16[80,640]{1,0:T(8,128)(2,1)S(1)} %pad_maximum_fusion.2), channel_id=1, source_target_pairs={{0,4},{4,8},{8,12},{1,5},{5,9},{9,13},{2,6},{6,10},{10,14},{3,7},{... | collective-permute-start | bytes 307208 | tf_op jit(solution)/shard_map/ppermute | solution.py:35
  15.4 5.4 %all-to-all-start = ((s32[4,256,1]{1,2,0:T(1,128)}), s32[4,256,1]{1,2,0:T(1,128)S(1)}, u32[]{:S(2)}, u32[]{:S(2)}) async-start(s32[4,256,1]{1,2,0:T(1,128)} %compare_select_fusion.1), calls=%async_computation | async-start | bytes 8192 | tf_op jit(solution)/shard_map/all_to_all | solution.py:132
  22.4 1.4 %fusion.135 = (f32[80,2303]{1,0:T(8,128)}, f32[80,2303]{1,0:T(8,128)}) fusion(f32[80,2304]{1,0:T(8,128)S(1)} %bitcast.120), kind=kLoop, calls=%fused_computation.219 | loop fusion | bytes 2947840 | tf_op jit(solution)/shard_map/slice | solution.py:76
  25.8 2.2 %fusion.6 = pred[256,2304]{1,0:T(32,128)(4,1)} fusion(s32[256]{0:T(256)S(1)} %get-tuple-element.62, s32[256]{0:T(256)S(1)} %get-tuple-element.63, s32[2304]{0:T(1024)S(1)} %get-tuple-element.66, s32[2304]{0:T(1024)S(1)} %get-tuple-element.67, s32[256]{0:T(256)S(1)} %get-tuple-element.61, s32[256]{0:T(256)S(1)} %get-tuple-element.64, ...), kind=kLoop, calls=%fused_computation.21 | loop fusion | flops 13565952 | bytes 635904 | tf_op jit(solution)/shard_map/and | solution.py:103
  33.9 2.8 %convolution_bitcast_fusion.2 = f32[80,2048]{1,0:T(8,128)S(1)} fusion(f32[80,80]{1,0:T(8,128)S(1)} %copy-done, f32[80,2048]{1,0:T(8,128)S(1)} %bitcast.125, f32[80,256]{1,0:T(8,128)S(1)} %slice_convert_fusion.3, f32[80,1792]{1,0:T(8,128)} %get-tuple-element.28, f32[80,1792]{1,0:T(8,128)} %get-tuple-element.27, f32[80,256]{1,0:T(8,128)S(1)} %slice_convert_fusion.2, ...), kind=kOutput, calls=%fused_computation.14 | convolution fusion | flops 159088640 | bytes 5272256 | tf_op jit(solution)/shard_map/dot_general | solution.py:85
  37.1 2.8 %gather_fusion.1 = f32[1024,80]{1,0:T(8,128)S(1)} fusion(f32[80,2048]{0,1:T(8,128)S(1)} %copy.97, s32[1024]{0:T(1024)S(1)} %broadcast_clamp_fusion), kind=kCustom, calls=%fused_computation.1 | custom fusion | bytes 659456 | tf_op jit(solution)/shard_map/jit(_take)/gather | solution.py:133
  40.3 1.5 %collective-permute-start.4 = (f32[80,256]{1,0:T(8,128)S(1)}, f32[80,256]{1,0:T(8,128)S(1)}, u32[]{:S(2)}, u32[]{:S(2)}) collective-permute-start(f32[80,256]{1,0:T(8,128)S(1)} %bitcast.157), channel_id=1, source_target_pairs={{0,4},{4,0},{8,12},{12,8},{1,5},{5,1},{9,13},{13,9},{2,6},{6,2},{1... | collective-permute-start | bytes 245768 | tf_op jit(solution)/shard_map/ppermute | solution.py:139
  41.9 2.1 %collective-permute-start.5 = (f32[80,256]{1,0:T(8,128)S(1)}, f32[80,256]{1,0:T(8,128)S(1)}, u32[]{:S(2)}, u32[]{:S(2)}) collective-permute-start(f32[80,256]{1,0:T(8,128)S(1)} %bitcast.158), channel_id=1, source_target_pairs={{0,8},{4,12},{8,0},{12,4},{1,9},{5,13},{9,1},{13,5},{2,10},{6,14},... | collective-permute-start | bytes 245768 | tf_op jit(solution)/shard_map/ppermute | solution.py:139
  45.7 1.5 %collective-permute-done.5 = f32[80,256]{1,0:T(8,128)S(1)} collective-permute-done((f32[80,256]{1,0:T(8,128)S(1)}, f32[80,256]{1,0:T(8,128)S(1)}, u32[]{:S(2)}, u32[]{:S(2)}) %collective-permute-start.5) | collective-permute-done | bytes 81952 | tf_op jit(solution)/shard_map/ppermute | solution.py:139
  47.2 2.1 %collective-permute-done.6 = f32[80,256]{1,0:T(8,128)S(1)} collective-permute-done((f32[80,256]{1,0:T(8,128)S(1)}, f32[80,256]{1,0:T(8,128)S(1)}, u32[]{:S(2)}, u32[]{:S(2)}) %collective-permute-start.6) | collective-permute-done | bytes 81952 | tf_op jit(solution)/shard_map/ppermute | solution.py:139
  51.4 2.8 %fusion.146 = (bf16[80,2304]{1,0:T(8,128)(2,1)S(1)}, f32[80,2304]{1,0:T(8,128)S(1)}) fusion(f32[80,80]{1,0:T(8,128)S(1)} %copy-done, f32[80,2304]{1,0:T(8,128)S(1)} %fusion.149, f32[80,2304]{1,0:T(8,128)S(1)} %bitcast.122, f32[80,1920]{1,0:T(8,128)} %get-tuple-element.23, f32[80,384]{1,0:T(8,128)S(1)} %copy-done.18, f32[80,384]{1,0:T(8,128)S(1)} %copy-done.19, ...), kind=kOutput, calls=%fused_computation.230 | convolution fusion | flops 180080640 | bytes 7052800 | tf_op jit(solution)/shard_map/dot_general | solution.py:85
  55.1 4.6 %collective-permute-start.9 = (bf16[80,6]{0,1:T(8,128)(2,1)S(1)}, bf16[80,6]{0,1:T(8,128)(2,1)S(1)}, u32[]{:S(2)}, u32[]{:S(2)}) collective-permute-start(bf16[80,6]{0,1:T(8,128)(2,1)S(1)} %bitcast.175), channel_id=1, source_target_pairs={{1,0},{2,1},{3,2},{5,4},{6,5},{7,6},{9,8},{10,9},{11,10},{13,12},{... | collective-permute-start | bytes 2888 | tf_op jit(solution)/shard_map/ppermute | solution.py:38
  59.9 2.6 %collective-permute-start.10 = (bf16[80,6]{0,1:T(8,128)(2,1)S(1)}, bf16[80,6]{0,1:T(8,128)(2,1)S(1)}, u32[]{:S(2)}, u32[]{:S(2)}) collective-permute-start(bf16[80,6]{0,1:T(8,128)(2,1)S(1)} %bitcast.173), channel_id=1, source_target_pairs={{0,1},{1,2},{2,3},{4,5},{5,6},{6,7},{8,9},{9,10},{10,11},{12,13},{... | collective-permute-start | bytes 2888 | tf_op jit(solution)/shard_map/ppermute | solution.py:37
  64.9 4.2 %collective-permute-start.8 = (bf16[80,384]{1,0:T(8,128)(2,1)S(1)}, bf16[80,384]{1,0:T(8,128)(2,1)S(1)}, u32[]{:S(2)}, u32[]{:S(2)}) collective-permute-start(bf16[80,384]{1,0:T(8,128)(2,1)S(1)} %bitcast.162), channel_id=1, source_target_pairs={{0,4},{4,8},{8,12},{1,5},{5,9},{9,13},{2,6},{6,10},{10,14},{3,7},{... | collective-permute-start | bytes 184328 | tf_op jit(solution)/shard_map/ppermute | solution.py:35
  73.3 1.3 %fusion.147 = (bf16[80,2304]{1,0:T(8,128)(2,1)S(1)}, f32[80,2304]{1,0:T(8,128)S(1)}) fusion(f32[80,80]{1,0:T(8,128)S(1)} %copy-done, f32[80,2304]{1,0:T(8,128)S(1)} %fusion.149, f32[80,2304]{1,0:T(8,128)S(1)} %get-tuple-element.52, f32[80,1920]{1,0:T(8,128)S(1)} %copy-done.14, f32[80,384]{1,0:T(8,128)S(1)} %convert_element_type.84, ...), kind=kOutput, calls=%fused_computation.231 | convolution fusion | flops 180080640 | bytes 7052800 | tf_op jit(solution)/shard_map/dot_general | solution.py:85
  75.6 2.3 %collective-permute-start.13 = (bf16[80,6]{0,1:T(8,128)(2,1)S(1)}, bf16[80,6]{0,1:T(8,128)(2,1)S(1)}, u32[]{:S(2)}, u32[]{:S(2)}) collective-permute-start(bf16[80,6]{0,1:T(8,128)(2,1)S(1)} %bitcast.176), channel_id=1, source_target_pairs={{1,0},{2,1},{3,2},{5,4},{6,5},{7,6},{9,8},{10,9},{11,10},{13,12},{... | collective-permute-start | bytes 2888 | tf_op jit(solution)/shard_map/ppermute | solution.py:38
  78.0 3.3 %collective-permute-start.14 = (bf16[80,6]{0,1:T(8,128)(2,1)S(1)}, bf16[80,6]{0,1:T(8,128)(2,1)S(1)}, u32[]{:S(2)}, u32[]{:S(2)}) collective-permute-start(bf16[80,6]{0,1:T(8,128)(2,1)S(1)} %bitcast.174), channel_id=1, source_target_pairs={{0,1},{1,2},{2,3},{4,5},{5,6},{6,7},{8,9},{9,10},{10,11},{12,13},{... | collective-permute-start | bytes 2888 | tf_op jit(solution)/shard_map/ppermute | solution.py:37
  82.9 4.0 %collective-permute-start.12 = (bf16[80,384]{1,0:T(8,128)(2,1)S(1)}, bf16[80,384]{1,0:T(8,128)(2,1)S(1)}, u32[]{:S(2)}, u32[]{:S(2)}) collective-permute-start(bf16[80,384]{1,0:T(8,128)(2,1)S(1)} %bitcast.163), channel_id=1, source_target_pairs={{0,4},{4,8},{8,12},{1,5},{5,9},{9,13},{2,6},{6,10},{10,14},{3,7},{... | collective-permute-start | bytes 184328 | tf_op jit(solution)/shard_map/ppermute | solution.py:35
  91.0 1.3 %fusion.148 = (bf16[2304,80]{0,1:T(8,128)(2,1)S(1)}, f32[2304,80]{0,1:T(8,128)S(1)}) fusion(f32[80,80]{1,0:T(8,128)S(1)} %copy-done, f32[80,2304]{1,0:T(8,128)S(1)} %fusion.149, f32[80,2304]{1,0:T(8,128)S(1)} %get-tuple-element.54, f32[80,1920]{1,0:T(8,128)S(1)} %copy-done.12, f32[80,384]{1,0:T(8,128)S(1)} %convert_element_type.89, ...), kind=kOutput, calls=%fused_computation.232 | convolution fusion | flops 180080640 | bytes 7052800 | tf_op jit(solution)/shard_map/dot_general | solution.py:85
  94.4 3.5 %all-to-all-start.1 = ((f32[80,4,256]{2,0,1:T(8,128)}), f32[80,4,256]{2,0,1:T(8,128)S(1)}, u32[]{:S(2)}, u32[]{:S(2)}) async-start(f32[80,4,256]{2,0,1:T(8,128)} %broadcast_select_fusion.1), calls=%async_computation.1 | async-start | bytes 655360 | tf_op jit(solution)/shard_map/all_to_all | solution.py:181
  98.6 9.6 %all-to-all-done.1 = f32[80,4,256]{2,0,1:T(8,128)S(1)} async-done(((f32[80,4,256]{2,0,1:T(8,128)}), f32[80,4,256]{2,0,1:T(8,128)S(1)}, u32[]{:S(2)}, u32[]{:S(2)}) %all-to-all-start.1) | async-done | bytes 327712 | tf_op jit(solution)/shard_map/all_to_all | solution.py:181
  108.5 6.3 %scatter_custom_fusion = f32[80,2048]{0,1:T(8,128)S(1)} fusion(s32[1024]{0:T(1024)S(1)} %bitcast.166, f32[1024,80]{1,0:T(8,128)S(1)} %copy.115, f32[]{:T(128)} %constant.113.clone.1), kind=kCustom, calls=%fused_computation.93 | custom fusion | flops 81920 | bytes 655364 | tf_op jit(solution)/shard_map/scatter-add | solution.py:182
  (196 shorter events, 37.9 us)
Async XLA Ops:
  0.6 33.3 %copy-start = (f32[80,80]{1,0:T(8,128)S(1)}, f32[80,80]{1,0:T(8,128)}, u32[]{:S(2)}) copy-start(f32[80,80]{1,0:T(8,128)} %param.16) | copy-start | bytes 76804
  0.6 9.4 %copy-start.16 = (bf16[80,8,256]{2,1,0:T(8,128)(2,1)S(1)}, bf16[80,8,256]{2,1,0:T(8,128)(2,1)}, u32[]{:S(2)}) copy-start(bf16[80,8,256]{2,1,0:T(8,128)(2,1)} %param.10) | copy-start | bytes 983044
  0.7 9.5 %copy-start.17 = (bf16[80,6,384]{2,0,1:T(8,128)(2,1)S(1)}, bf16[80,6,384]{2,0,1:T(8,128)(2,1)}, u32[]{:S(2)}) copy-start(bf16[80,6,384]{2,0,1:T(8,128)(2,1)} %param.11) | copy-start | bytes 1105924
  2.0 12.7 %copy-start.26 = (s32[1,1,256,1]{2,3,1,0:T(1,128)S(1)}, s32[1,1,256,1]{2,3,1,0:T(1,128)}, u32[]{:S(2)}) copy-start(s32[1,1,256,1]{2,3,1,0:T(1,128)} %param.17) | copy-start | bytes 3076
  2.0 12.8 %copy-start.27 = (s32[1,1,256]{2,1,0:T(1,128)S(1)}, s32[1,1,256]{2,1,0:T(1,128)}, u32[]{:S(2)}) copy-start(s32[1,1,256]{2,1,0:T(1,128)} %param.18) | copy-start | bytes 3076
  3.3 24.8 %collective-permute-start.2 = (bf16[80,14]{0,1:T(8,128)(2,1)S(1)}, bf16[80,14]{0,1:T(8,128)(2,1)S(1)}, u32[]{:S(2)}, u32[]{:S(2)}) collective-permute-start(bf16[80,14]{0,1:T(8,128)(2,1)S(1)} %pad_maximum_fusion.3), channel_id=1, source_target_pairs={{1,0},{2,1},{3,2},{5,4},{6,5},{7,6},{9,8},{10,9},{11,10},{13,12},{... | collective-permute-start | bytes 6728 | tf_op jit(solution)/shard_map/ppermute | solution.py:38
  5.5 22.6 %collective-permute-start.3 = (bf16[80,14]{0,1:T(8,128)(2,1)S(1)}, bf16[80,14]{0,1:T(8,128)(2,1)S(1)}, u32[]{:S(2)}, u32[]{:S(2)}) collective-permute-start(bf16[80,14]{0,1:T(8,128)(2,1)S(1)} %pad_maximum_fusion.4), channel_id=1, source_target_pairs={{0,1},{1,2},{2,3},{4,5},{5,6},{6,7},{8,9},{9,10},{10,11},{12,13},{... | collective-permute-start | bytes 6728 | tf_op jit(solution)/shard_map/ppermute | solution.py:37
  10.2 23.0 %collective-permute-start.1 = (bf16[80,640]{1,0:T(8,128)(2,1)S(1)}, bf16[80,640]{1,0:T(8,128)(2,1)S(1)}, u32[]{:S(2)}, u32[]{:S(2)}) collective-permute-start(bf16[80,640]{1,0:T(8,128)(2,1)S(1)} %pad_maximum_fusion.2), channel_id=1, source_target_pairs={{0,4},{4,8},{8,12},{1,5},{5,9},{9,13},{2,6},{6,10},{10,14},{3,7},{... | collective-permute-start | bytes 307208 | tf_op jit(solution)/shard_map/ppermute | solution.py:35
  13.5 19.8 %collective-permute-start = (bf16[80,640]{1,0:T(8,128)(2,1)S(1)}, bf16[80,640]{1,0:T(8,128)(2,1)S(1)}, u32[]{:S(2)}, u32[]{:S(2)}) collective-permute-start(bf16[80,640]{1,0:T(8,128)(2,1)S(1)} %pad_maximum_fusion.1), channel_id=1, source_target_pairs={{4,0},{8,4},{12,8},{5,1},{9,5},{13,9},{6,2},{10,6},{14,10},{7,3},{... | collective-permute-start | bytes 307208 | tf_op jit(solution)/shard_map/ppermute | solution.py:36
  15.4 17.8 %all-to-all-start = ((s32[4,256,1]{1,2,0:T(1,128)}), s32[4,256,1]{1,2,0:T(1,128)S(1)}, u32[]{:S(2)}, u32[]{:S(2)}) async-start(s32[4,256,1]{1,2,0:T(1,128)} %compare_select_fusion.1), calls=%async_computation | async-start | bytes 8192 | tf_op jit(solution)/shard_map/all_to_all | solution.py:132
  40.1 4.8 %copy-start.23 = (bf16[80,640]{1,0:T(8,128)(2,1)S(1)}, bf16[80,640]{1,0:T(8,128)(2,1)}, u32[]{:S(2)}) copy-start(bf16[80,640]{1,0:T(8,128)(2,1)} %copy-done.22) | copy-start | bytes 307204
  40.3 5.4 %collective-permute-start.4 = (f32[80,256]{1,0:T(8,128)S(1)}, f32[80,256]{1,0:T(8,128)S(1)}, u32[]{:S(2)}, u32[]{:S(2)}) collective-permute-start(f32[80,256]{1,0:T(8,128)S(1)} %bitcast.157), channel_id=1, source_target_pairs={{0,4},{4,0},{8,12},{12,8},{1,5},{5,1},{9,13},{13,9},{2,6},{6,2},{1... | collective-permute-start | bytes 245768 | tf_op jit(solution)/shard_map/ppermute | solution.py:139
  41.9 5.3 %collective-permute-start.5 = (f32[80,256]{1,0:T(8,128)S(1)}, f32[80,256]{1,0:T(8,128)S(1)}, u32[]{:S(2)}, u32[]{:S(2)}) collective-permute-start(f32[80,256]{1,0:T(8,128)S(1)} %bitcast.158), channel_id=1, source_target_pairs={{0,8},{4,12},{8,0},{12,4},{1,9},{5,13},{9,1},{13,5},{2,10},{6,14},... | collective-permute-start | bytes 245768 | tf_op jit(solution)/shard_map/ppermute | solution.py:139
  44.1 5.2 %collective-permute-start.6 = (f32[80,256]{1,0:T(8,128)S(1)}, f32[80,256]{1,0:T(8,128)S(1)}, u32[]{:S(2)}, u32[]{:S(2)}) collective-permute-start(f32[80,256]{1,0:T(8,128)S(1)} %bitcast.159), channel_id=1, source_target_pairs={{0,12},{4,8},{8,4},{12,0},{1,13},{5,9},{9,5},{13,1},{2,14},{6,10},... | collective-permute-start | bytes 245768 | tf_op jit(solution)/shard_map/ppermute | solution.py:139
  44.9 5.1 %copy-start.4 = (pred[256,2304]{1,0:T(32,128)(4,1)S(1)}, pred[256,2304]{1,0:T(32,128)(4,1)}, u32[]{:S(2)}) copy-start(pred[256,2304]{1,0:T(32,128)(4,1)} %fusion.6) | copy-start | bytes 1769476
  55.1 15.2 %collective-permute-start.9 = (bf16[80,6]{0,1:T(8,128)(2,1)S(1)}, bf16[80,6]{0,1:T(8,128)(2,1)S(1)}, u32[]{:S(2)}, u32[]{:S(2)}) collective-permute-start(bf16[80,6]{0,1:T(8,128)(2,1)S(1)} %bitcast.175), channel_id=1, source_target_pairs={{1,0},{2,1},{3,2},{5,4},{6,5},{7,6},{9,8},{10,9},{11,10},{13,12},{... | collective-permute-start | bytes 2888 | tf_op jit(solution)/shard_map/ppermute | solution.py:38
  59.9 11.6 %collective-permute-start.10 = (bf16[80,6]{0,1:T(8,128)(2,1)S(1)}, bf16[80,6]{0,1:T(8,128)(2,1)S(1)}, u32[]{:S(2)}, u32[]{:S(2)}) collective-permute-start(bf16[80,6]{0,1:T(8,128)(2,1)S(1)} %bitcast.173), channel_id=1, source_target_pairs={{0,1},{1,2},{2,3},{4,5},{5,6},{6,7},{8,9},{9,10},{10,11},{12,13},{... | collective-permute-start | bytes 2888 | tf_op jit(solution)/shard_map/ppermute | solution.py:37
  63.6 8.3 %collective-permute-start.7 = (bf16[80,384]{1,0:T(8,128)(2,1)S(1)}, bf16[80,384]{1,0:T(8,128)(2,1)S(1)}, u32[]{:S(2)}, u32[]{:S(2)}) collective-permute-start(bf16[80,384]{1,0:T(8,128)(2,1)S(1)} %bitcast.160), channel_id=1, source_target_pairs={{4,0},{8,4},{12,8},{5,1},{9,5},{13,9},{6,2},{10,6},{14,10},{7,3},{... | collective-permute-start | bytes 184328 | tf_op jit(solution)/shard_map/ppermute | solution.py:36
  64.9 7.0 %collective-permute-start.8 = (bf16[80,384]{1,0:T(8,128)(2,1)S(1)}, bf16[80,384]{1,0:T(8,128)(2,1)S(1)}, u32[]{:S(2)}, u32[]{:S(2)}) collective-permute-start(bf16[80,384]{1,0:T(8,128)(2,1)S(1)} %bitcast.162), channel_id=1, source_target_pairs={{0,4},{4,8},{8,12},{1,5},{5,9},{9,13},{2,6},{6,10},{10,14},{3,7},{... | collective-permute-start | bytes 184328 | tf_op jit(solution)/shard_map/ppermute | solution.py:35
  75.6 12.4 %collective-permute-start.13 = (bf16[80,6]{0,1:T(8,128)(2,1)S(1)}, bf16[80,6]{0,1:T(8,128)(2,1)S(1)}, u32[]{:S(2)}, u32[]{:S(2)}) collective-permute-start(bf16[80,6]{0,1:T(8,128)(2,1)S(1)} %bitcast.176), channel_id=1, source_target_pairs={{1,0},{2,1},{3,2},{5,4},{6,5},{7,6},{9,8},{10,9},{11,10},{13,12},{... | collective-permute-start | bytes 2888 | tf_op jit(solution)/shard_map/ppermute | solution.py:38
  78.0 11.3 %collective-permute-start.14 = (bf16[80,6]{0,1:T(8,128)(2,1)S(1)}, bf16[80,6]{0,1:T(8,128)(2,1)S(1)}, u32[]{:S(2)}, u32[]{:S(2)}) collective-permute-start(bf16[80,6]{0,1:T(8,128)(2,1)S(1)} %bitcast.174), channel_id=1, source_target_pairs={{0,1},{1,2},{2,3},{4,5},{5,6},{6,7},{8,9},{9,10},{10,11},{12,13},{... | collective-permute-start | bytes 2888 | tf_op jit(solution)/shard_map/ppermute | solution.py:37
  81.6 8.2 %collective-permute-start.11 = (bf16[80,384]{1,0:T(8,128)(2,1)S(1)}, bf16[80,384]{1,0:T(8,128)(2,1)S(1)}, u32[]{:S(2)}, u32[]{:S(2)}) collective-permute-start(bf16[80,384]{1,0:T(8,128)(2,1)S(1)} %bitcast.161), channel_id=1, source_target_pairs={{4,0},{8,4},{12,8},{5,1},{9,5},{13,9},{6,2},{10,6},{14,10},{7,3},{... | collective-permute-start | bytes 184328 | tf_op jit(solution)/shard_map/ppermute | solution.py:36
  82.9 6.9 %collective-permute-start.12 = (bf16[80,384]{1,0:T(8,128)(2,1)S(1)}, bf16[80,384]{1,0:T(8,128)(2,1)S(1)}, u32[]{:S(2)}, u32[]{:S(2)}) collective-permute-start(bf16[80,384]{1,0:T(8,128)(2,1)S(1)} %bitcast.163), channel_id=1, source_target_pairs={{0,4},{4,8},{8,12},{1,5},{5,9},{9,13},{2,6},{6,10},{10,14},{3,7},{... | collective-permute-start | bytes 184328 | tf_op jit(solution)/shard_map/ppermute | solution.py:35
  94.4 13.8 %all-to-all-start.1 = ((f32[80,4,256]{2,0,1:T(8,128)}), f32[80,4,256]{2,0,1:T(8,128)S(1)}, u32[]{:S(2)}, u32[]{:S(2)}) async-start(f32[80,4,256]{2,0,1:T(8,128)} %broadcast_select_fusion.1), calls=%async_computation.1 | async-start | bytes 655360 | tf_op jit(solution)/shard_map/all_to_all | solution.py:181
  (23 other events, 33.8 us)
